TPU v7x, 256 devices: a whole 4x4x8 slice. The times are simulated.
256 devices in a mesh: region: 8 (over z), row: 32 (over y, x, core).
Axes of the slice: x: 4, y: 4, z: 8, core: 2. Of those that a mesh axis runs over, the one named last changes fastest.
Arguments:
- state0: float32 [32, 131072], P(None, ('region', 'row')), may hold values from -6 to 6
- drive: bfloat16 [32, 131072], P(None, ('region', 'row')), may hold values from -6 to 6
- cotangent: float32 [32, 131072], P(None, ('region', 'row')), may hold values from -6 to 6
- excitatory: int32 [131072], P(('region', 'row')), may hold values 0 or 1
- tile_vals: bfloat16 [1024, 24, 128, 128], P(('region', 'row')), may hold values from 0.0039978027 to 0.039794922
- tile_cols: int32 [1024, 24], P(('region', 'row')), may hold values from 0 to 159
- tile_count: int32 [1024], P(('region', 'row')), may hold values from 1 to 24, as said below
- boundary_rows: int32 [8, 32, 8, 16], P('region', 'row'), may hold values from 0 to 511, as said below
- u_factor: bfloat16 [32, 131072], P(None, ('region', 'row')), may hold values from -1 to 1
- v_factor: bfloat16 [32, 131072], P(None, ('region', 'row')), may hold values from -0.015625 to 0.015625
Outputs:
- final_state: float32 [32, 131072], P(None, ('region', 'row'))
- grad_u: float32 [32, 131072], P(None, ('region', 'row'))
- grad_v: float32 [32, 131072], P(None, ('region', 'row'))
Inputs may be any that keep to these rules, and one draw needn't show every extreme that they name: tile_count[q] tiles of row tile q are live; its tiles j >= tile_count[q] take no part; the most, 24, is reached in every draw. `boundary_rows`: the 16 rows of one list are distinct. tile_cols[q, j] numbers a tile of 128 extended columns of the group of row tile q.
All inputs are finite; a program needn't handle non-finite values. No bound on the sum of `excitatory` on one device may be relied on, other than what follows from the above.
Results may differ from a plain program's by a relative error of at most 0.0055.
Values may be sent and summed in bfloat16 or wider, within the bound.
No kernel may reach another device: no remote copies, remote signals or barrier semaphores. Data moves between devices by JAX's collectives and lax.ppermute only.
A program may use at most 64 MiB of HBM per device.

v0:
```python
import jax
import jax.numpy as jnp
from jax import lax
from jax.sharding import Mesh
from jax.sharding import PartitionSpec as P

STEPS = 4
ROW = ("row_0", "row_1", "row_2")
REGION_ROW = ("region", "row_0", "row_1", "row_2")
leak = 0.5


def apply_tiles(ext_cols, flat_cols, live_tiles, flat_tiles, row_tiles):
    batch_rows, span_cols = ext_cols.shape
    blocks = ext_cols.reshape(batch_rows, span_cols // 128, 128)[:, flat_cols, :]
    blocks = jnp.where(live_tiles[None, :, None], blocks, jnp.zeros((), blocks.dtype))
    product = jnp.einsum("bsk,sik->bsi", blocks, flat_tiles, preferred_element_type=jnp.float32)
    summed = product.reshape(batch_rows, row_tiles, -1, 128).sum(axis=2)
    return summed.reshape(batch_rows, row_tiles * 128)


def from_each_region(x, me):
    everyone = lax.all_gather(x, "region", axis=0, tiled=False)
    mine = lax.dynamic_index_in_dim(everyone, me, axis=2, keepdims=False)
    return jnp.moveaxis(mine, 0, 1).reshape(x.shape[0], -1)


def local(
    state0,
    drive,
    cotangent,
    excitatory,
    tile_vals,
    tile_cols,
    tile_count,
    boundary_rows,
    u_factor,
    v_factor,
):
    lanes = lax.axis_size(ROW)
    groups = lax.axis_size("region")
    me = lax.axis_index("region")
    own_rows = state0.shape[1]
    own_tiles = own_rows // 128
    row_tiles = tile_vals.shape[0]
    chosen = boundary_rows.reshape(-1)
    bound_cols = chosen.shape[0]
    bound_tiles = bound_cols // 128
    per_lane = own_tiles + bound_tiles
    lane_of = tile_cols // per_lane
    at_lane = tile_cols % per_lane
    remapped = jnp.where(
        at_lane < own_tiles,
        lane_of * own_tiles + at_lane,
        lanes * own_tiles + lane_of * bound_tiles + at_lane - own_tiles,
    )
    flat_cols = remapped.reshape(-1)
    live_grid = jnp.arange(tile_cols.shape[1], dtype=jnp.int32)[None, :] < tile_count[:, None]
    live_tiles = live_grid.reshape(-1)
    flat_tiles = tile_vals.reshape(-1, 128, 128)
    polarity = (2 * excitatory - 1).astype(jnp.float32)
    state = state0
    saved = []
    for moment in range(STEPS):
        rates = jnp.tanh(state)
        signed = (polarity * rates).astype(jnp.bfloat16)
        batch_rows = signed.shape[0]
        gathered_own = lax.all_gather(signed, ROW, axis=1, tiled=True)
        outgoing = jnp.take(signed, chosen, axis=1).reshape(batch_rows, groups, -1)
        incoming = from_each_region(outgoing, me)
        latent = lax.psum(
            jnp.dot(signed, v_factor.T, preferred_element_type=jnp.float32), REGION_ROW
        )
        gathered_border = lax.all_gather(incoming, ROW, axis=1, tiled=True)
        gathered = jnp.concatenate([gathered_own, gathered_border], axis=1)
        synaptic = apply_tiles(gathered, flat_cols, live_tiles, flat_tiles, row_tiles)
        latent_b = latent.astype(jnp.bfloat16)
        lowrank = jnp.dot(latent_b, u_factor, preferred_element_type=jnp.float32)
        saved.append((rates, signed, latent_b))
        state = state + leak * (-state + synaptic + lowrank + drive.astype(jnp.float32))
    grad_u = jnp.zeros((u_factor.shape[0], own_rows), jnp.float32)
    grad_v = jnp.zeros((v_factor.shape[0], own_rows), jnp.float32)
    adjoint = cotangent
    for moment in reversed(range(STEPS)):
        rates, signed, latent_b = saved[moment]
        scaled_b = (leak * adjoint).astype(jnp.bfloat16)
        coeffs = lax.psum(
            jnp.dot(scaled_b, u_factor.T, preferred_element_type=jnp.float32), REGION_ROW
        )
        coeffs_b = coeffs.astype(jnp.bfloat16)
        batch_rows = scaled_b.shape[0]
        spread = jnp.einsum(
            "bri,rjik->brjk",
            scaled_b.reshape(batch_rows, row_tiles, 128),
            tile_vals,
            preferred_element_type=jnp.float32,
        )
        spread = jnp.where(live_grid[None, :, :, None], spread, 0.0)
        columns = jnp.zeros((batch_rows, lanes * per_lane, 128), jnp.float32)
        columns = columns.at[:, flat_cols, :].add(spread.reshape(batch_rows, -1, 128))
        rounded = columns.astype(jnp.bfloat16).astype(jnp.float32)
        own_cols = rounded[:, : lanes * own_tiles].reshape(batch_rows, -1)
        border_cols = rounded[:, lanes * own_tiles :].reshape(batch_rows, -1)
        border = lax.psum_scatter(border_cols, ROW, scatter_dimension=1, tiled=True)
        returned = from_each_region(border.reshape(batch_rows, groups, -1), me)
        own_part = lax.psum_scatter(own_cols, ROW, scatter_dimension=1, tiled=True)
        through = own_part.at[:, chosen].add(returned)
        total_signed = through + jnp.dot(coeffs_b, v_factor, preferred_element_type=jnp.float32)
        grad_u = grad_u + jnp.dot(latent_b.T, scaled_b, preferred_element_type=jnp.float32)
        grad_v = grad_v + jnp.dot(coeffs_b.T, signed, preferred_element_type=jnp.float32)
        adjoint = (1.0 - leak) * adjoint + (1.0 - rates * rates) * polarity * total_signed
    return (state, grad_u, grad_v)


def solution(mesh):
    finer = Mesh(
        mesh.devices.reshape(mesh.shape["region"], 4, 4, 2), ("region", "row_0", "row_1", "row_2")
    )
    in_specs = (
        P(None, REGION_ROW),
        P(None, REGION_ROW),
        P(None, REGION_ROW),
        P(REGION_ROW),
        P(REGION_ROW, None, None, None),
        P(REGION_ROW, None),
        P(REGION_ROW),
        P("region", ROW, None, None),
        P(None, REGION_ROW),
        P(None, REGION_ROW),
    )
    out_specs = (P(None, REGION_ROW), P(None, REGION_ROW), P(None, REGION_ROW))
    return jax.shard_map(local, mesh=finer, in_specs=in_specs, out_specs=out_specs, check_vma=False)
```

profile of v0, /device:TPU:1, one launch (start us, length us, event | category | flops | bytes accessed | tf_op | source)
XLA Modules:
  0.0 1002.2 jit_solution(16985678666152582495)
XLA Ops:
  8.1 1.5 multiply_convert_fusion.4
  12.2 23.3 %all_gather.46 = bf16[8,32,8,16]{1,3,2,0:T(8,128)(2,1)S(1)} all-gather(bf16[1,32,8,16]{1,3,2,0:T(8,128)(2,1)S(1)} %bitcast.256), channel_id=1, replica_groups=mesh['region'=8,'row_0'=4,'row_1'=4,'row_2'=2] {'region'}, dimensions={0}, use_global_device_ids=true | all-gather | bytes 73728 | tf_op jit(solution)/shard_map/all_gather | solution.py:23
  38.0 81.1 %psum.56 = bf16[32,32]{1,0:T(8,128)(2,1)S(1)} all-reduce(f32[32,32]{1,0:T(8,128)S(1)} %fusion.61), channel_id=1, replica_groups=mesh['region'=8,'row_0'=4,'row_1'=4,'row_2'=2] {'region','row_0','row_1'..., use_global_device_ids=true, to_apply=%region_1.3 | all-reduce | flops 1024 | bytes 6144 | tf_op jit(solution)/shard_map/psum | solution.py:71
  119.2 24.4 %all_gather.47 = bf16[32,4096]{1,0:T(8,128)(2,1)S(1)} all-gather(bf16[32,128]{1,0:T(8,128)(2,1)S(1)} %copy.91), channel_id=1, replica_groups=mesh['region'=8,'row_0'=4,'row_1'=4,'row_2'=2] {'row_0','row_1','row_2'}, dimensions={1}, use_global_device_ids=true | all-gather | bytes 270336 | tf_op jit(solution)/shard_map/all_gather | solution.py:74
  143.6 2.5 copy_bitcast_fusion.6
  146.1 2.9 gather_fusion
  149.0 4.1 fusion.18
  153.2 1.5 reduce_sum.36
  155.6 1.7 convolution_select_fusion.2
  157.3 1.8 broadcast.101.clone
  159.1 13.2 %scatter_fusion = f32[32,160,128]{2,0,1:T(8,128)} fusion(f32[32,160,128]{2,0,1:T(8,128)} %broadcast.101.clone, s32[96]{0:T(128)S(1)} %fusion.53, f32[96,32,128]{2,1,0:T(8,128)} %bitcast.243), kind=kCustom, calls=%fused_computation.8 | custom fusion | flops 393216 | bytes 4718976 | tf_op jit(solution)/shard_map/scatter-add | solution.py:100
  172.4 2.0 convert_convert_fusion.2
  174.3 1.5 copy-done.1
  176.7 3.1 copy_bitcast_fusion.2
  181.5 19.1 %all_gather.49 = bf16[8,32,8,16]{1,3,2,0:T(8,128)(2,1)S(1)} all-gather(bf16[1,32,8,16]{1,3,2,0:T(8,128)(2,1)S(1)} %bitcast.257), channel_id=1, replica_groups=mesh['region'=8,'row_0'=4,'row_1'=4,'row_2'=2] {'region'}, dimensions={0}, use_global_device_ids=true | all-gather | bytes 73728 | tf_op jit(solution)/shard_map/all_gather | solution.py:23
  201.4 77.0 %psum.57 = bf16[32,32]{1,0:T(8,128)(2,1)} all-reduce(f32[32,32]{1,0:T(8,128)S(1)} %fusion.62), channel_id=1, replica_groups=mesh['region'=8,'row_0'=4,'row_1'=4,'row_2'=2] {'region','row_0','row_1'..., use_global_device_ids=true, to_apply=%region_3.5 | all-reduce | flops 1024 | bytes 6144 | tf_op jit(solution)/shard_map/psum | solution.py:71
  278.4 24.3 %all_gather.50 = bf16[32,4096]{1,0:T(8,128)(2,1)S(1)} all-gather(bf16[32,128]{1,0:T(8,128)(2,1)} %copy.95), channel_id=1, replica_groups=mesh['region'=8,'row_0'=4,'row_1'=4,'row_2'=2] {'row_0','row_1','row_2'}, dimensions={1}, use_global_device_ids=true | all-gather | bytes 270336 | tf_op jit(solution)/shard_map/all_gather | solution.py:74
  302.8 2.5 copy_bitcast_fusion.5
  305.3 3.0 gather_fusion.1
  308.4 4.2 fusion.16
  312.5 1.5 reduce_sum.37
  317.1 19.2 %all_gather.57 = f32[8,32,8,16]{1,3,2,0:T(8,128)S(1)} all-gather(f32[1,32,8,16]{1,3,2,0:T(8,128)S(1)} %bitcast.249), channel_id=1, replica_groups=mesh['region'=8,'row_0'=4,'row_1'=4,'row_2'=2] {'region'}, dimensions={0}, use_global_device_ids=true | all-gather | bytes 147456 | tf_op jit(solution)/shard_map/all_gather | solution.py:23
  338.7 19.3 %all_gather.52 = bf16[8,32,8,16]{1,3,2,0:T(8,128)(2,1)S(1)} all-gather(bf16[1,32,8,16]{1,3,2,0:T(8,128)(2,1)S(1)} %bitcast.258), channel_id=1, replica_groups=mesh['region'=8,'row_0'=4,'row_1'=4,'row_2'=2] {'region'}, dimensions={0}, use_global_device_ids=true | all-gather | bytes 73728 | tf_op jit(solution)/shard_map/all_gather | solution.py:23
  360.9 83.6 %all-reduce.1 = (bf16[32,32]{1,0:T(8,128)(2,1)}, bf16[32,32]{1,0:T(8,128)(2,1)S(1)}) all-reduce(f32[32,32]{1,0:T(8,128)S(1)} %fusion.63, f32[32,32]{1,0:T(8,128)} %fusion.65), channel_id=1, replica_groups=mesh['region'=8,'row_0'=4,'row_1'=4,'row_2'=2] {'region','row_0','row_1'..., use_global_device_ids=true, to_apply=%region_5.7 | all-reduce | flops 2048 | bytes 12288 | tf_op jit(solution)/shard_map/psum | solution.py:71
  445.1 1.6 convolution_add_fusion.8
  447.7 1.9 scatter_fusion.1
  450.3 24.4 %all_gather.53 = bf16[32,4096]{1,0:T(8,128)(2,1)S(1)} all-gather(bf16[32,128]{1,0:T(8,128)(2,1)} %copy.99), channel_id=1, replica_groups=mesh['region'=8,'row_0'=4,'row_1'=4,'row_2'=2] {'row_0','row_1','row_2'}, dimensions={1}, use_global_device_ids=true | all-gather | bytes 270336 | tf_op jit(solution)/shard_map/all_gather | solution.py:74
  474.7 2.5 copy_bitcast_fusion.4
  477.2 3.0 gather_fusion.2
  480.2 4.1 fusion.14
  484.4 1.5 reduce_sum.38
  487.4 2.3 convolution_select_fusion.1
  489.7 1.8 broadcast.101.clone.1
  491.6 13.2 %scatter_fusion.2 = f32[32,160,128]{2,0,1:T(8,128)} fusion(f32[32,160,128]{2,0,1:T(8,128)} %broadcast.101.clone.1, s32[96]{0:T(128)S(1)} %copy-done.35, f32[96,32,128]{2,1,0:T(8,128)} %bitcast.244), kind=kCustom, calls=%fused_computation.10 | custom fusion | flops 393216 | bytes 4718976 | tf_op jit(solution)/shard_map/scatter-add | solution.py:100
  504.7 2.0 convert_convert_fusion.1
  506.7 1.5 copy-done.2
  509.1 3.1 copy_bitcast_fusion.1
  512.4 73.7 %psum.61 = bf16[32,32]{1,0:T(8,128)(2,1)S(1)} all-reduce(f32[32,32]{1,0:T(8,128)S(1)} %fusion.66), channel_id=1, replica_groups=mesh['region'=8,'row_0'=4,'row_1'=4,'row_2'=2] {'region','row_0','row_1'..., use_global_device_ids=true, to_apply=%region_15.17 | all-reduce | flops 1024 | bytes 6144 | tf_op jit(solution)/shard_map/psum | solution.py:87
  586.2 1.7 reduce-scatter.13.cloned.1.call-done
  588.7 21.2 %all_gather.58 = f32[8,32,8,16]{1,3,2,0:T(8,128)S(1)} all-gather(f32[1,32,8,16]{1,3,2,0:T(8,128)S(1)} %bitcast.250), channel_id=1, replica_groups=mesh['region'=8,'row_0'=4,'row_1'=4,'row_2'=2] {'region'}, dimensions={0}, use_global_device_ids=true | all-gather | bytes 147456 | tf_op jit(solution)/shard_map/all_gather | solution.py:23
  610.5 67.1 %reduce-scatter.11.cloned.1.call-done = f32[32,512]{1,0:T(8,128)} async-done(((f32[32,16384]{1,0:T(8,128)}), f32[32,512]{1,0:T(8,128)}) %reduce-scatter.11.cloned.1.call-update) | async-done | bytes 65552 | tf_op jit(solution)/shard_map/reduce_scatter | solution.py:106
  677.6 1.6 convolution_add_fusion.6
  680.1 1.7 scatter_fusion.3
  683.5 2.3 convolution_select_fusion
  685.8 1.8 broadcast.101
  687.6 13.2 %scatter_fusion.4 = f32[32,160,128]{2,0,1:T(8,128)} fusion(f32[32,160,128]{2,0,1:T(8,128)} %broadcast.101, s32[96]{0:T(128)S(1)} %copy-done.36, f32[96,32,128]{2,1,0:T(8,128)} %bitcast.242), kind=kCustom, calls=%fused_computation.12 | custom fusion | flops 393216 | bytes 4718976 | tf_op jit(solution)/shard_map/scatter-add | solution.py:100
  700.8 2.0 convert_convert_fusion
  702.8 1.5 copy-done.3
  705.2 3.1 copy_bitcast_fusion
  710.0 20.6 %all_gather.55 = bf16[8,32,8,16]{1,3,2,0:T(8,128)(2,1)S(1)} all-gather(bf16[1,32,8,16]{1,3,2,0:T(8,128)(2,1)S(1)} %bitcast.255), channel_id=1, replica_groups=mesh['region'=8,'row_0'=4,'row_1'=4,'row_2'=2] {'region'}, dimensions={0}, use_global_device_ids=true | all-gather | bytes 73728 | tf_op jit(solution)/shard_map/all_gather | solution.py:23
  732.6 31.8 %all_gather.56 = bf16[32,4096]{1,0:T(8,128)(2,1)S(1)} all-gather(bf16[32,128]{1,0:T(8,128)(2,1)} %copy.103), channel_id=1, replica_groups=mesh['region'=8,'row_0'=4,'row_1'=4,'row_2'=2] {'row_0','row_1','row_2'}, dimensions={1}, use_global_device_ids=true | all-gather | bytes 270336 | tf_op jit(solution)/shard_map/all_gather | solution.py:74
  766.8 1.6 convolution_add_fusion.2
  768.4 2.5 copy_bitcast_fusion.3
  770.9 3.0 gather_fusion.3
  774.0 4.1 fusion.12
  778.1 2.1 reduce_sum.39
  780.3 74.4 %psum.62 = bf16[32,32]{1,0:T(8,128)(2,1)S(1)} all-reduce(f32[32,32]{1,0:T(8,128)S(1)} %fusion.67), channel_id=1, replica_groups=mesh['region'=8,'row_0'=4,'row_1'=4,'row_2'=2] {'region','row_0','row_1'..., use_global_device_ids=true, to_apply=%region_20.22 | all-reduce | flops 1024 | bytes 6144 | tf_op jit(solution)/shard_map/psum | solution.py:87
  856.4 19.5 %all_gather.59 = f32[8,32,8,16]{1,3,2,0:T(8,128)S(1)} all-gather(f32[1,32,8,16]{1,3,2,0:T(8,128)S(1)} %bitcast.251), channel_id=1, replica_groups=mesh['region'=8,'row_0'=4,'row_1'=4,'row_2'=2] {'region'}, dimensions={0}, use_global_device_ids=true | all-gather | bytes 147456 | tf_op jit(solution)/shard_map/all_gather | solution.py:23
  876.5 28.5 %reduce-scatter.15.cloned.1.call-done = f32[32,512]{1,0:T(8,128)} async-done(((f32[32,16384]{1,0:T(8,128)}), f32[32,512]{1,0:T(8,128)}) %reduce-scatter.15.cloned.1.call-update) | async-done | bytes 65552 | tf_op jit(solution)/shard_map/reduce_scatter | solution.py:106
  905.0 1.6 convolution_add_fusion.4
  907.6 1.7 scatter_fusion.5
  911.1 77.4 %all-reduce = (bf16[32,32]{1,0:T(8,128)(2,1)S(1)}, bf16[32,32]{1,0:T(8,128)(2,1)S(1)}) all-reduce(f32[32,32]{1,0:T(8,128)} %fusion.64, f32[32,32]{1,0:T(8,128)S(1)} %fusion.68), channel_id=1, replica_groups=mesh['region'=8,'row_0'=4,'row_1'=4,'row_2'=2] {'region','row_0','row_1'..., use_global_device_ids=true, to_apply=%region_7.9 | all-reduce | flops 2048 | bytes 12288 | tf_op jit(solution)/shard_map/psum | solution.py:71
  992.1 1.7 convolution_add_fusion
  993.7 1.6 fusion.2
  (173 shorter events, 43.3 us)
Async XLA Ops:
  7.2 141.8 %copy-start = (bf16[4,24,128,128]{3,2,1,0:T(8,128)(2,1)S(1)}, bf16[4,24,128,128]{3,2,1,0:T(8,128)(2,1)}, u32[]{:S(2)}) copy-start(bf16[4,24,128,128]{3,2,1,0:T(8,128)(2,1)} %param.16) | copy-start | bytes 9437188
  7.2 136.4 %all-gather.5.cloned.1.call-start = ((), (), s32[]{:S(2)}) async-start(), calls=%async_computation.6 | async-start | bytes 1081344 | tf_op jit(solution)/shard_map/all_gather | solution.py:68
  9.6 293.2 %all-gather.7.cloned.1.call-start = ((), (), s32[]{:S(2)}) async-start(), calls=%async_computation.7 | async-start | bytes 1081344 | tf_op jit(solution)/shard_map/all_gather | solution.py:68
  12.1 169.3 %copy-start.31 = (pred[128]{0:T(512)(128)(4,1)}, pred[128]{0:T(512)(128)(4,1)S(1)}, u32[]{:S(2)}) copy-start(pred[128]{0:T(512)(128)(4,1)S(1)} %compare_and_fusion) | copy-start | bytes 388
  37.1 118.5 %copy-start.37 = (pred[4,24]{1,0:T(4,128)(4,1)}, pred[4,24]{1,0:T(4,128)(4,1)S(1)}, u32[]{:S(2)}) copy-start(pred[4,24]{1,0:T(4,128)(4,1)S(1)} %iota_compare_fusion) | copy-start | bytes 292
  37.1 111.8 %copy-start.28 = (pred[96]{0:T(512)(128)(4,1)}, pred[96]{0:T(512)(128)(4,1)S(1)}, u32[]{:S(2)}) copy-start(pred[96]{0:T(512)(128)(4,1)S(1)} %lt.81) | copy-start | bytes 292
  143.5 15.6 %copy-start.34 = (s32[96]{0:T(128)}, s32[96]{0:T(128)S(1)}, u32[]{:S(2)}) copy-start(s32[96]{0:T(128)S(1)} %fusion.53) | copy-start | bytes 1156
  143.5 5.4 copy-start.27
  149.0 5.7 copy-start.4
  149.0 5.7 copy-start.10
  149.0 5.7 copy-start.18
  149.0 6.5 copy-start.21
  155.5 160.8 %reduce-scatter.9.cloned.1.call-start = ((), (), s32[]{:S(2)}) async-start(), calls=%async_computation.11 | async-start | bytes 540672 | tf_op jit(solution)/shard_map/reduce_scatter | solution.py:104
  155.6 1.7 copy-start.13
  174.3 1.5 copy-start.1
  176.7 267.8 %reduce-scatter.7.cloned.1.call-start = ((), (), s32[]{:S(2)}) async-start(), calls=%async_computation.10 | async-start | bytes 2162688 | tf_op jit(solution)/shard_map/reduce_scatter | solution.py:106
  179.8 0.8 copy-start.6
  179.8 21.5 %copy-start.5 = (bf16[32,512]{1,0:T(8,128)(2,1)S(1)}, bf16[32,512]{1,0:T(8,128)(2,1)}, u32[]{:S(2)}) copy-start(bf16[32,512]{1,0:T(8,128)(2,1)} %param.21) | copy-start | bytes 98308
  179.8 294.9 %all-gather.9.cloned.1.call-start = ((), (), s32[]{:S(2)}) async-start(), calls=%async_computation.8 | async-start | bytes 1081344 | tf_op jit(solution)/shard_map/all_gather | solution.py:68
  302.8 5.6 copy-start.29
  308.4 5.7 copy-start.9
  308.4 5.7 copy-start.11
  308.4 5.7 copy-start.23
  308.4 6.6 copy-start.26
  308.4 7.2 copy-start.14
  312.5 26.0 %copy-start.32 = (pred[128]{0:T(512)(128)(4,1)S(1)}, pred[128]{0:T(512)(128)(4,1)}, u32[]{:S(2)}) copy-start(pred[128]{0:T(512)(128)(4,1)} %copy-done.31) | copy-start | bytes 388
  314.9 273.0 %reduce-scatter.13.cloned.1.call-start = ((), (), s32[]{:S(2)}) async-start(), calls=%async_computation.13 | async-start | bytes 540672 | tf_op jit(solution)/shard_map/reduce_scatter | solution.py:104
  444.5 0.6 copy-start.25
  480.2 5.6 copy-start.12
  480.2 5.6 copy-start.20
  480.2 5.7 copy-start.22
  487.4 24.9 %copy-start.15 = (bf16[32,512]{1,0:T(8,128)(2,1)}, bf16[32,512]{1,0:T(8,128)(2,1)S(1)}, u32[]{:S(2)}) copy-start(bf16[32,512]{1,0:T(8,128)(2,1)S(1)} %get-tuple-element.8) | copy-start | bytes 98308
  489.7 1.9 copy-start.35
  506.7 1.5 copy-start.2
  509.1 168.5 %reduce-scatter.11.cloned.1.call-start = ((), (), s32[]{:S(2)}) async-start(), calls=%async_computation.12 | async-start | bytes 2162688 | tf_op jit(solution)/shard_map/reduce_scatter | solution.py:106
  512.2 256.2 %all-gather.11.cloned.1.call-start = ((), (), s32[]{:S(2)}) async-start(), calls=%async_computation.9 | async-start | bytes 1081344 | tf_op jit(solution)/shard_map/all_gather | solution.py:68
  586.1 91.5 %copy-start.24 = (bf16[32,32]{1,0:T(8,128)(2,1)}, bf16[32,32]{1,0:T(8,128)(2,1)S(1)}, u32[]{:S(2)}) copy-start(bf16[32,32]{1,0:T(8,128)(2,1)S(1)} %psum.61) | copy-start | bytes 6148
  586.2 269.4 %reduce-scatter.17.cloned.1.call-start = ((), (), s32[]{:S(2)}) async-start(), calls=%async_computation.15 | async-start | bytes 540672 | tf_op jit(solution)/shard_map/reduce_scatter | solution.py:104
  683.5 2.3 copy-start.16
  685.8 1.9 copy-start.36
  702.8 1.5 copy-start.3
  705.2 199.8 %reduce-scatter.15.cloned.1.call-start = ((), (), s32[]{:S(2)}) async-start(), calls=%async_computation.14 | async-start | bytes 2162688 | tf_op jit(solution)/shard_map/reduce_scatter | solution.py:106
  708.3 0.8 copy-start.8
  708.3 1.6 copy-start.33
  768.4 5.5 copy-start.30
  773.9 6.3 copy-start.17
  773.9 80.8 %copy-start.7 = (bf16[32,512]{1,0:T(8,128)(2,1)S(1)}, bf16[32,512]{1,0:T(8,128)(2,1)}, u32[]{:S(2)}) copy-start(bf16[32,512]{1,0:T(8,128)(2,1)} %get-tuple-element.11) | copy-start | bytes 98308
  774.0 80.8 %copy-start.19 = (f32[32,512]{1,0:T(8,128)S(1)}, f32[32,512]{1,0:T(8,128)}, u32[]{:S(2)}) copy-start(f32[32,512]{1,0:T(8,128)} %convolution_add_fusion.2) | copy-start | bytes 196612
  778.1 129.5 %copy-start.38 = (s32[128]{0:T(128)S(1)}, s32[128]{0:T(128)}, u32[]{:S(2)}) copy-start(s32[128]{0:T(128)} %fusion.54) | copy-start | bytes 1540
Sparse Core Ops, SparseCore 0:
  10.5 52.4 all-gather.4
  155.6 44.2 all-gather.6
  203.6 81.8 reduce-scatter.8
  289.2 85.9 reduce-scatter.6
  377.6 49.4 all-gather.8
  509.2 78.6 reduce-scatter.12
  591.7 85.8 reduce-scatter.10
  680.1 49.4 all-gather.10
  733.3 82.0 reduce-scatter.16
  819.1 85.8 reduce-scatter.14
where the time goes:
time: 1010 us; the launch traced here: 1000 us
  blocking collectives  714 us (71%)
  waiting for transfers between devices  97.5 us (10%)
  other arithmetic  74.2 us (7%)
  local copies, waits for them, and re-layouts  56 us (6%)
  matrix products  45.3 us (4%)
  between operations  14.6 us (1%)
    psum x4, blocking collectives, local(): lax.psum(jnp.dot(signed, v_factor.T, preferred_element_type=jnp.float32),...  319 us
    psum x2, blocking collectives, local(): lax.psum(jnp.dot(scaled_b, u_factor.T, preferred_element_type=jnp.float32...  148 us
    all_gather x7, blocking collectives, from_each_region(): everyone = lax.all_gather(x, 'region', axis=0, tiled=False)  142 us
    all_gather x4, blocking collectives, local(): gathered_border = lax.all_gather(incoming, ROW, axis=1, tiled=True)  105 us
    reduce_scatter x3, waiting for transfers between devices, local(): own_part = lax.psum_scatter(own_cols, ROW, scatter_dimension=1, tiled=True)  95.6 us
    scatter-add x3, other arithmetic, local(): columns.at[:, flat_cols, :].add(spread.reshape(batch_rows, -1, 128))  39.6 us
  transfers between devices with their start and end apart: 10, of which 3 were waited for; matrix products, arithmetic and copies ran while one was open for 11% of the time, Pallas kernels for 0%

commit v1 on v0

--- a/solution.py
+++ b/solution.py
@@ -84,8 +84,11 @@
     for moment in reversed(range(STEPS)):
         rates, signed, latent_b = saved[moment]
         scaled_b = (leak * adjoint).astype(jnp.bfloat16)
-        coeffs = lax.psum(
-            jnp.dot(scaled_b, u_factor.T, preferred_element_type=jnp.float32), REGION_ROW
+        coeffs = jnp.sum(
+            lax.all_gather(
+                jnp.dot(scaled_b, u_factor.T, preferred_element_type=jnp.float32), REGION_ROW
+            ),
+            axis=0,
         )
         coeffs_b = coeffs.astype(jnp.bfloat16)
         batch_rows = scaled_b.shape[0]

time: 1010 us -> 1450 us (1.44)
  waiting for transfers between devices: 97.5 us -> 686 us
  blocking collectives: 714 us -> 564 us
    all_gather x0 -> x4, waiting for transfers between devices: none -> 317 us  [local(): lax.all_gather(jnp.dot(scaled_b, u_factor.T, preferred_element_type=jnp.f...]
    reduce_scatter x3, waiting for transfers between devices: 95.6 us -> 248 us  [local(): own_part = lax.psum_scatter(own_cols, ROW, scatter_dimension=1, tiled=True)]
    psum x2 -> x0, blocking collectives: 148 us -> none  [local(): lax.psum(jnp.dot(scaled_b, u_factor.T, preferred_element_type=jnp.float32...]
    reduce_scatter x3, waiting for transfers between devices: 1.68 us -> 76.2 us  [local(): border = lax.psum_scatter(border_cols, ROW, scatter_dimension=1, tiled=True)]
    all_gather x4, waiting for transfers between devices: 0.03 us -> 43.2 us  [local(): gathered_own = lax.all_gather(signed, ROW, axis=1, tiled=True)]
  transfers between devices with their start and end apart: 10 -> 14, of which waited for: 3 -> 9; matrix products, arithmetic and copies ran while one was open for 11% -> 7% of each run, Pallas kernels for 0% -> 0%
where the time goes in v1:
time: 1450 us; the launch traced here: 1440 us
  waiting for transfers between devices  686 us (47%)
  blocking collectives  564 us (39%)
  other arithmetic  83.4 us (6%)
  local copies, waits for them, and re-layouts  52.8 us (4%)
  matrix products  42.8 us (3%)
  between operations  14.5 us (1%)
    psum x4, blocking collectives, local(): lax.psum(jnp.dot(signed, v_factor.T, preferred_element_type=jnp.float32),...  322 us
    all_gather x4, waiting for transfers between devices, local(): lax.all_gather(jnp.dot(scaled_b, u_factor.T, preferred_element_type=jnp.f...  317 us
    reduce_scatter x3, waiting for transfers between devices, local(): own_part = lax.psum_scatter(own_cols, ROW, scatter_dimension=1, tiled=True)  248 us
    all_gather x7, blocking collectives, from_each_region(): everyone = lax.all_gather(x, 'region', axis=0, tiled=False)  145 us
    all_gather x4, blocking collectives, local(): gathered_border = lax.all_gather(incoming, ROW, axis=1, tiled=True)  97.1 us
    reduce_scatter x3, waiting for transfers between devices, local(): border = lax.psum_scatter(border_cols, ROW, scatter_dimension=1, tiled=True)  76.2 us
    all_gather x4, waiting for transfers between devices, local(): gathered_own = lax.all_gather(signed, ROW, axis=1, tiled=True)  43.2 us
    scatter-add x3, other arithmetic, local(): columns.at[:, flat_cols, :].add(spread.reshape(batch_rows, -1, 128))  39.7 us
  transfers between devices with their start and end apart: 14, of which 9 were waited for; matrix products, arithmetic and copies ran while one was open for 7% of the time, Pallas kernels for 0%

profile of v1, /device:TPU:1, one launch (start us, length us, event | category | flops | bytes accessed | tf_op | source)
XLA Modules:
  0.0 1444.4 jit_solution(14764983206433964775)
XLA Ops:
  8.1 1.5 multiply_convert_fusion.4
  12.2 23.3 %all_gather.70 = bf16[8,32,8,16]{1,3,2,0:T(8,128)(2,1)S(1)} all-gather(bf16[1,32,8,16]{1,3,2,0:T(8,128)(2,1)S(1)} %bitcast.264), channel_id=1, replica_groups=mesh['region'=8,'row_0'=4,'row_1'=4,'row_2'=2] {'region'}, dimensions={0}, use_global_device_ids=true | all-gather | bytes 73728 | tf_op jit(solution)/shard_map/all_gather | solution.py:23
  38.1 81.2 %psum.28 = bf16[32,32]{1,0:T(8,128)(2,1)S(1)} all-reduce(f32[32,32]{1,0:T(8,128)S(1)} %fusion.61), channel_id=1, replica_groups=mesh['region'=8,'row_0'=4,'row_1'=4,'row_2'=2] {'region','row_0','row_1'..., use_global_device_ids=true, to_apply=%region_1.3 | all-reduce | flops 1024 | bytes 6144 | tf_op jit(solution)/shard_map/psum | solution.py:71
  119.3 24.3 %all_gather.71 = bf16[32,4096]{1,0:T(8,128)(2,1)S(1)} all-gather(bf16[32,128]{1,0:T(8,128)(2,1)S(1)} %copy.91), channel_id=1, replica_groups=mesh['region'=8,'row_0'=4,'row_1'=4,'row_2'=2] {'row_0','row_1','row_2'}, dimensions={1}, use_global_device_ids=true | all-gather | bytes 270336 | tf_op jit(solution)/shard_map/all_gather | solution.py:74
  143.6 2.5 copy_bitcast_fusion.6
  146.2 2.9 gather_fusion
  149.1 4.1 fusion.18
  155.7 1.7 convolution_select_fusion.2
  157.4 1.8 broadcast.101.clone
  159.2 13.2 scatter_fusion
  172.5 2.0 convert_convert_fusion.2
  177.7 3.1 copy_bitcast_fusion.2
  182.5 18.7 %all_gather.73 = bf16[8,32,8,16]{1,3,2,0:T(8,128)(2,1)S(1)} all-gather(bf16[1,32,8,16]{1,3,2,0:T(8,128)(2,1)S(1)} %bitcast.265), channel_id=1, replica_groups=mesh['region'=8,'row_0'=4,'row_1'=4,'row_2'=2] {'region'}, dimensions={0}, use_global_device_ids=true | all-gather | bytes 73728 | tf_op jit(solution)/shard_map/all_gather | solution.py:23
  202.0 77.4 %psum.29 = bf16[32,32]{1,0:T(8,128)(2,1)S(1)} all-reduce(f32[32,32]{1,0:T(8,128)S(1)} %fusion.62), channel_id=1, replica_groups=mesh['region'=8,'row_0'=4,'row_1'=4,'row_2'=2] {'region','row_0','row_1'..., use_global_device_ids=true, to_apply=%region_3.5 | all-reduce | flops 1024 | bytes 6144 | tf_op jit(solution)/shard_map/psum | solution.py:71
  279.4 24.4 %all_gather.74 = bf16[32,4096]{1,0:T(8,128)(2,1)S(1)} all-gather(bf16[32,128]{1,0:T(8,128)(2,1)} %copy.95), channel_id=1, replica_groups=mesh['region'=8,'row_0'=4,'row_1'=4,'row_2'=2] {'row_0','row_1','row_2'}, dimensions={1}, use_global_device_ids=true | all-gather | bytes 270336 | tf_op jit(solution)/shard_map/all_gather | solution.py:74
  303.8 2.6 copy_bitcast_fusion.5
  306.4 2.9 gather_fusion.1
  309.3 4.2 fusion.16
  316.8 20.3 %all_gather.83 = f32[8,32,8,16]{1,3,2,0:T(8,128)S(1)} all-gather(f32[1,32,8,16]{1,3,2,0:T(8,128)S(1)} %bitcast.257), channel_id=1, replica_groups=mesh['region'=8,'row_0'=4,'row_1'=4,'row_2'=2] {'region'}, dimensions={0}, use_global_device_ids=true | all-gather | bytes 147456 | tf_op jit(solution)/shard_map/all_gather | solution.py:23
  337.7 68.6 %all-gather.21.cloned.1.call-done = f32[8192,32]{1,0:T(8,128)} async-done(((f32[32,32]{1,0:T(8,128)}), f32[8192,32]{1,0:T(8,128)}) %all-gather.21.cloned.1.call-update) | async-done | bytes 1048592 | tf_op jit(solution)/shard_map/all_gather | solution.py:88
  406.3 2.5 reduce_sum.76
  408.9 82.8 %reduce-scatter.7.cloned.1.call-done = f32[32,512]{1,0:T(8,128)} async-done(((f32[32,16384]{1,0:T(8,128)}), f32[32,512]{1,0:T(8,128)}) %reduce-scatter.7.cloned.1.call-update) | async-done | bytes 65552 | tf_op jit(solution)/shard_map/reduce_scatter | solution.py:109
  491.7 1.6 convolution_add_fusion.8
  494.2 1.7 scatter_fusion.1
  498.5 20.5 %all_gather.76 = bf16[8,32,8,16]{1,3,2,0:T(8,128)(2,1)S(1)} all-gather(bf16[1,32,8,16]{1,3,2,0:T(8,128)(2,1)S(1)} %bitcast.266), channel_id=1, replica_groups=mesh['region'=8,'row_0'=4,'row_1'=4,'row_2'=2] {'region'}, dimensions={0}, use_global_device_ids=true | all-gather | bytes 73728 | tf_op jit(solution)/shard_map/all_gather | solution.py:23
  521.9 81.9 %psum.30 = bf16[32,32]{1,0:T(8,128)(2,1)S(1)} all-reduce(f32[32,32]{1,0:T(8,128)S(1)} %fusion.63), channel_id=1, replica_groups=mesh['region'=8,'row_0'=4,'row_1'=4,'row_2'=2] {'region','row_0','row_1'..., use_global_device_ids=true, to_apply=%region_5.7 | all-reduce | flops 1024 | bytes 6144 | tf_op jit(solution)/shard_map/psum | solution.py:71
  603.8 22.9 %all_gather.77 = bf16[32,4096]{1,0:T(8,128)(2,1)S(1)} all-gather(bf16[32,128]{1,0:T(8,128)(2,1)} %copy.99), channel_id=1, replica_groups=mesh['region'=8,'row_0'=4,'row_1'=4,'row_2'=2] {'row_0','row_1','row_2'}, dimensions={1}, use_global_device_ids=true | all-gather | bytes 270336 | tf_op jit(solution)/shard_map/all_gather | solution.py:74
  626.7 2.5 copy_bitcast_fusion.4
  629.3 2.9 gather_fusion.2
  632.2 4.1 fusion.14
  638.7 2.3 convolution_select_fusion.1
  641.0 1.8 broadcast.101.clone.1
  642.8 13.2 scatter_fusion.2
  656.0 2.0 convert_convert_fusion.1
  661.3 3.1 copy_bitcast_fusion.1
  664.5 76.2 %reduce-scatter.13.cloned.1.call-done = f32[32,128]{1,0:T(8,128)} async-done(((f32[32,4096]{1,0:T(8,128)}), f32[32,128]{1,0:T(8,128)}) %reduce-scatter.13.cloned.1.call-update) | async-done | bytes 16400 | tf_op jit(solution)/shard_map/reduce_scatter | solution.py:107
  741.5 21.6 %all_gather.86 = f32[8,32,8,16]{1,3,2,0:T(8,128)S(1)} all-gather(f32[1,32,8,16]{1,3,2,0:T(8,128)S(1)} %bitcast.258), channel_id=1, replica_groups=mesh['region'=8,'row_0'=4,'row_1'=4,'row_2'=2] {'region'}, dimensions={0}, use_global_device_ids=true | all-gather | bytes 147456 | tf_op jit(solution)/shard_map/all_gather | solution.py:23
  763.7 97.4 %all-gather.23.cloned.1.call-done = f32[8192,32]{1,0:T(8,128)} async-done(((f32[32,32]{1,0:T(8,128)}), f32[8192,32]{1,0:T(8,128)}) %all-gather.23.cloned.1.call-update) | async-done | bytes 1048592 | tf_op jit(solution)/shard_map/all_gather | solution.py:88
  861.1 2.5 reduce_sum.77
  863.6 82.9 %reduce-scatter.11.cloned.1.call-done = f32[32,512]{1,0:T(8,128)} async-done(((f32[32,16384]{1,0:T(8,128)}), f32[32,512]{1,0:T(8,128)}) %reduce-scatter.11.cloned.1.call-update) | async-done | bytes 65552 | tf_op jit(solution)/shard_map/reduce_scatter | solution.py:109
  946.5 1.6 convolution_add_fusion.6
  949.1 1.7 scatter_fusion.3
  952.4 2.3 convolution_select_fusion
  954.7 1.8 broadcast.101
  956.6 13.2 scatter_fusion.4
  969.8 2.0 convert_convert_fusion
  975.0 3.1 copy_bitcast_fusion
  980.0 20.1 %all_gather.79 = bf16[8,32,8,16]{1,3,2,0:T(8,128)(2,1)S(1)} all-gather(bf16[1,32,8,16]{1,3,2,0:T(8,128)(2,1)S(1)} %bitcast.263), channel_id=1, replica_groups=mesh['region'=8,'row_0'=4,'row_1'=4,'row_2'=2] {'region'}, dimensions={0}, use_global_device_ids=true | all-gather | bytes 73728 | tf_op jit(solution)/shard_map/all_gather | solution.py:23
  1000.4 81.9 %psum.31 = bf16[32,32]{1,0:T(8,128)(2,1)} all-reduce(f32[32,32]{1,0:T(8,128)S(1)} %fusion.64), channel_id=1, replica_groups=mesh['region'=8,'row_0'=4,'row_1'=4,'row_2'=2] {'region','row_0','row_1'..., use_global_device_ids=true, to_apply=%region_7.9 | all-reduce | flops 1024 | bytes 6144 | tf_op jit(solution)/shard_map/psum | solution.py:71
  1082.3 25.4 %all_gather.80 = bf16[32,4096]{1,0:T(8,128)(2,1)} all-gather(bf16[32,128]{1,0:T(8,128)(2,1)S(1)} %copy.103), channel_id=1, replica_groups=mesh['region'=8,'row_0'=4,'row_1'=4,'row_2'=2] {'row_0','row_1','row_2'}, dimensions={1}, use_global_device_ids=true | all-gather | bytes 270336 | tf_op jit(solution)/shard_map/all_gather | solution.py:74
  1109.3 20.5 %all_gather.89 = f32[8,32,8,16]{1,3,2,0:T(8,128)S(1)} all-gather(f32[1,32,8,16]{1,3,2,0:T(8,128)S(1)} %bitcast.259), channel_id=1, replica_groups=mesh['region'=8,'row_0'=4,'row_1'=4,'row_2'=2] {'region'}, dimensions={0}, use_global_device_ids=true | all-gather | bytes 147456 | tf_op jit(solution)/shard_map/all_gather | solution.py:23
  1130.4 48.2 %all-gather.25.cloned.1.call-done = f32[8192,32]{1,0:T(8,128)} async-done(((f32[32,32]{1,0:T(8,128)}), f32[8192,32]{1,0:T(8,128)}) %all-gather.25.cloned.1.call-update) | async-done | bytes 1048592 | tf_op jit(solution)/shard_map/all_gather | solution.py:88
  1178.6 2.5 reduce_sum.78
  1181.2 82.8 %reduce-scatter.15.cloned.1.call-done = f32[32,512]{1,0:T(8,128)} async-done(((f32[32,16384]{1,0:T(8,128)}), f32[32,512]{1,0:T(8,128)}) %reduce-scatter.15.cloned.1.call-update) | async-done | bytes 65552 | tf_op jit(solution)/shard_map/reduce_scatter | solution.py:109
  1263.9 1.6 convolution_add_fusion.4
  1266.5 1.9 scatter_fusion.5
  1272.8 43.1 %all-gather.19.cloned.1.call-done = bf16[32,16384]{1,0:T(8,128)(2,1)} async-done(((bf16[32,512]{1,0:T(8,128)(2,1)}), bf16[32,16384]{1,0:T(8,128)(2,1)}) %all-gather.19.cloned.1.call-update) | async-done | bytes 1048592 | tf_op jit(solution)/shard_map/all_gather | solution.py:68
  1315.9 2.6 copy_bitcast_fusion.3
  1318.6 2.9 gather_fusion.3
  1321.5 4.2 fusion.12
  1325.7 1.5 reduce_sum.75
  1327.2 1.6 fusion.2
  1331.6 103.0 %all-gather.27.cloned.1.call-done = f32[8192,32]{1,0:T(8,128)} async-done(((f32[32,32]{1,0:T(8,128)}), f32[8192,32]{1,0:T(8,128)}) %all-gather.27.cloned.1.call-update) | async-done | bytes 1048592 | tf_op jit(solution)/shard_map/all_gather | solution.py:88
  1434.6 2.5 reduce_sum.79
  (203 shorter events, 50.5 us)
Async XLA Ops:
  7.2 141.9 %copy-start = (bf16[4,24,128,128]{3,2,1,0:T(8,128)(2,1)S(1)}, bf16[4,24,128,128]{3,2,1,0:T(8,128)(2,1)}, u32[]{:S(2)}) copy-start(bf16[4,24,128,128]{3,2,1,0:T(8,128)(2,1)} %param.16) | copy-start | bytes 9437188
  7.2 136.4 %all-gather.13.cloned.1.call-start = ((), (), s32[]{:S(2)}) async-start(), calls=%async_computation.6 | async-start | bytes 1081344 | tf_op jit(solution)/shard_map/all_gather | solution.py:68
  9.6 294.2 %all-gather.15.cloned.1.call-start = ((), (), s32[]{:S(2)}) async-start(), calls=%async_computation.7 | async-start | bytes 1081344 | tf_op jit(solution)/shard_map/all_gather | solution.py:68
  11.3 170.4 %copy-start.34 = (s32[1024]{0:T(1024)}, s32[1024]{0:T(1024)S(1)}, u32[]{:S(2)}) copy-start(s32[1024]{0:T(1024)S(1)} %pad_clamp_fusion.1) | copy-start | bytes 12292
  12.1 26.0 %copy-start.38 = (pred[128]{0:T(512)(128)(4,1)}, pred[128]{0:T(512)(128)(4,1)S(1)}, u32[]{:S(2)}) copy-start(pred[128]{0:T(512)(128)(4,1)S(1)} %compare_and_fusion) | copy-start | bytes 388
  37.1 118.6 %copy-start.45 = (pred[4,24]{1,0:T(4,128)(4,1)}, pred[4,24]{1,0:T(4,128)(4,1)S(1)}, u32[]{:S(2)}) copy-start(pred[4,24]{1,0:T(4,128)(4,1)S(1)} %iota_compare_fusion) | copy-start | bytes 292
  37.2 111.9 %copy-start.35 = (pred[96]{0:T(512)(128)(4,1)}, pred[96]{0:T(512)(128)(4,1)S(1)}, u32[]{:S(2)}) copy-start(pred[96]{0:T(512)(128)(4,1)S(1)} %lt.81) | copy-start | bytes 292
  119.3 35.5 %copy-start.31 = (bf16[32,32]{1,0:T(8,128)(2,1)}, bf16[32,32]{1,0:T(8,128)(2,1)S(1)}, u32[]{:S(2)}) copy-start(bf16[32,32]{1,0:T(8,128)(2,1)S(1)} %psum.28) | copy-start | bytes 6148
  143.6 15.6 %copy-start.42 = (s32[96]{0:T(128)}, s32[96]{0:T(128)S(1)}, u32[]{:S(2)}) copy-start(s32[96]{0:T(128)S(1)} %fusion.53) | copy-start | bytes 1156
  149.0 5.7 copy-start.4
  149.0 5.7 copy-start.12
  149.1 5.7 copy-start.20
  149.1 6.6 copy-start.23
  155.6 160.4 %reduce-scatter.9.cloned.1.call-start = ((), (), s32[]{:S(2)}) async-start(), calls=%async_computation.11 | async-start | bytes 540672 | tf_op jit(solution)/shard_map/reduce_scatter | solution.py:107
  155.7 21.2 %copy-start.16 = (bf16[32,512]{1,0:T(8,128)(2,1)}, bf16[32,512]{1,0:T(8,128)(2,1)S(1)}, u32[]{:S(2)}) copy-start(bf16[32,512]{1,0:T(8,128)(2,1)S(1)} %multiply_convert_fusion.5) | copy-start | bytes 98308
  174.4 1.5 copy-start.1
  176.8 229.5 %all-gather.21.cloned.1.call-start = ((), (), s32[]{:S(2)}) async-start(), calls=%async_computation.16 | async-start | bytes 4210688 | tf_op jit(solution)/shard_map/all_gather | solution.py:88
  177.7 314.0 %reduce-scatter.7.cloned.1.call-start = ((), (), s32[]{:S(2)}) async-start(), calls=%async_computation.10 | async-start | bytes 2162688 | tf_op jit(solution)/shard_map/reduce_scatter | solution.py:109
  180.8 0.8 copy-start.7
  180.8 1.6 copy-start.39
  180.8 21.0 %copy-start.5 = (bf16[32,512]{1,0:T(8,128)(2,1)S(1)}, bf16[32,512]{1,0:T(8,128)(2,1)}, u32[]{:S(2)}) copy-start(bf16[32,512]{1,0:T(8,128)(2,1)} %param.21) | copy-start | bytes 98308
  180.9 445.9 %all-gather.17.cloned.1.call-start = ((), (), s32[]{:S(2)}) async-start(), calls=%async_computation.8 | async-start | bytes 1081344 | tf_op jit(solution)/shard_map/all_gather | solution.py:68
  279.4 35.6 %copy-start.32 = (bf16[32,32]{1,0:T(8,128)(2,1)}, bf16[32,32]{1,0:T(8,128)(2,1)S(1)}, u32[]{:S(2)}) copy-start(bf16[32,32]{1,0:T(8,128)(2,1)S(1)} %psum.29) | copy-start | bytes 6148
  303.8 5.5 copy-start.36
  309.3 5.7 copy-start.11
  309.3 5.7 copy-start.13
  309.3 6.5 copy-start.33
  315.8 424.8 %reduce-scatter.13.cloned.1.call-start = ((), (), s32[]{:S(2)}) async-start(), calls=%async_computation.13 | async-start | bytes 540672 | tf_op jit(solution)/shard_map/reduce_scatter | solution.py:107
  316.0 178.3 %copy-start.46 = (s32[128]{0:T(128)}, s32[128]{0:T(128)S(1)}, u32[]{:S(2)}) copy-start(s32[128]{0:T(128)S(1)} %fusion.54) | copy-start | bytes 1540
  406.3 92.0 %copy-start.40 = (pred[128]{0:T(512)(128)(4,1)S(1)}, pred[128]{0:T(512)(128)(4,1)}, u32[]{:S(2)}) copy-start(pred[128]{0:T(512)(128)(4,1)} %copy-done.38) | copy-start | bytes 388
  408.9 82.8 %copy-start.25 = (bf16[32,32]{1,0:T(8,128)(2,1)}, bf16[32,32]{1,0:T(8,128)(2,1)S(1)}, u32[]{:S(2)}) copy-start(bf16[32,32]{1,0:T(8,128)(2,1)S(1)} %reduce_sum.76) | copy-start | bytes 6148
  632.2 5.7 copy-start.14
  632.2 5.7 copy-start.22
  632.2 5.7 copy-start.24
  638.6 21.8 %copy-start.17 = (bf16[32,512]{1,0:T(8,128)(2,1)}, bf16[32,512]{1,0:T(8,128)(2,1)S(1)}, u32[]{:S(2)}) copy-start(bf16[32,512]{1,0:T(8,128)(2,1)S(1)} %get-tuple-element.4) | copy-start | bytes 98308
  641.0 1.8 copy-start.43
  658.0 1.5 copy-start.2
  660.4 200.7 %all-gather.23.cloned.1.call-start = ((), (), s32[]{:S(2)}) async-start(), calls=%async_computation.17 | async-start | bytes 4210688 | tf_op jit(solution)/shard_map/all_gather | solution.py:88
  661.2 285.3 %reduce-scatter.11.cloned.1.call-start = ((), (), s32[]{:S(2)}) async-start(), calls=%async_computation.12 | async-start | bytes 2162688 | tf_op jit(solution)/shard_map/reduce_scatter | solution.py:109
  664.4 444.1 %reduce-scatter.17.cloned.1.call-start = ((), (), s32[]{:S(2)}) async-start(), calls=%async_computation.15 | async-start | bytes 540672 | tf_op jit(solution)/shard_map/reduce_scatter | solution.py:107
  863.6 82.9 %copy-start.27 = (bf16[32,32]{1,0:T(8,128)(2,1)}, bf16[32,32]{1,0:T(8,128)(2,1)S(1)}, u32[]{:S(2)}) copy-start(bf16[32,32]{1,0:T(8,128)(2,1)S(1)} %reduce_sum.77) | copy-start | bytes 6148
  952.4 21.8 %copy-start.18 = (bf16[32,512]{1,0:T(8,128)(2,1)}, bf16[32,512]{1,0:T(8,128)(2,1)S(1)}, u32[]{:S(2)}) copy-start(bf16[32,512]{1,0:T(8,128)(2,1)S(1)} %fusion.59) | copy-start | bytes 98308
  954.7 1.8 copy-start.44
  971.8 1.5 copy-start.3
  974.2 204.5 %all-gather.25.cloned.1.call-start = ((), (), s32[]{:S(2)}) async-start(), calls=%async_computation.18 | async-start | bytes 4210688 | tf_op jit(solution)/shard_map/all_gather | solution.py:88
  975.0 289.0 %reduce-scatter.15.cloned.1.call-start = ((), (), s32[]{:S(2)}) async-start(), calls=%async_computation.14 | async-start | bytes 2162688 | tf_op jit(solution)/shard_map/reduce_scatter | solution.py:109
  978.1 0.8 copy-start.10
  978.1 1.8 copy-start.41
  978.1 129.6 %copy-start.26 = (bf16[32,32]{1,0:T(8,128)(2,1)S(1)}, bf16[32,32]{1,0:T(8,128)(2,1)}, u32[]{:S(2)}) copy-start(bf16[32,32]{1,0:T(8,128)(2,1)} %copy-done.25) | copy-start | bytes 6148
  978.2 337.7 %all-gather.19.cloned.1.call-start = ((), (), s32[]{:S(2)}) async-start(), calls=%async_computation.9 | async-start | bytes 1081344 | tf_op jit(solution)/shard_map/all_gather | solution.py:68
  978.9 455.6 %all-gather.27.cloned.1.call-start = ((), (), s32[]{:S(2)}) async-start(), calls=%async_computation.19 | async-start | bytes 4210688 | tf_op jit(solution)/shard_map/all_gather | solution.py:88
  1181.2 82.8 %copy-start.29 = (bf16[32,32]{1,0:T(8,128)(2,1)}, bf16[32,32]{1,0:T(8,128)(2,1)S(1)}, u32[]{:S(2)}) copy-start(bf16[32,32]{1,0:T(8,128)(2,1)S(1)} %reduce_sum.78) | copy-start | bytes 6148
  1272.8 48.7 %copy-start.37 = (pred[96]{0:T(512)(128)(4,1)S(1)}, pred[96]{0:T(512)(128)(4,1)}, u32[]{:S(2)}) copy-start(pred[96]{0:T(512)(128)(4,1)} %copy-done.35) | copy-start | bytes 292
  1321.5 5.7 copy-start.15
  1321.5 7.3 copy-start.9
  1321.5 7.3 copy-start.21
  1321.5 7.3 copy-start.28
  1325.7 3.4 copy-start.19
  1325.7 4.2 copy-start.8
  1325.7 4.2 copy-start.30
  1434.6 2.5 copy-start.6
Sparse Core Ops, SparseCore 0:
  10.5 52.4 all-gather.12
  155.7 44.2 all-gather.14
  203.7 81.9 reduce-scatter.8
  289.7 116.5 all-gather.20
  410.0 81.6 reduce-scatter.6
  494.0 49.5 all-gather.16
  660.5 80.0 reduce-scatter.12
  744.2 116.7 all-gather.22
  864.9 81.5 reduce-scatter.10
  974.3 84.0 reduce-scatter.16
  1062.0 116.5 all-gather.24
  1182.3 81.5 reduce-scatter.14
  1266.4 49.4 all-gather.18
  1319.9 114.5 all-gather.26
